TPU v7x, 32 devices: a whole 2x2x4 slice. The times are simulated.
32 devices in a mesh: groups: 2 (over y), section: 4 (over x, core), filt: 4 (over z).
Axes of the slice: x: 2, y: 2, z: 4, core: 2. Of those that a mesh axis runs over, the one named last changes fastest.
Arguments:
- volumes: bfloat16 [16, 256, 4, 2, 128], P('groups', 'filt'), parts along dimension 0, may hold values from -6 to 6
- weights: bfloat16 [4, 256, 27, 256], P('section', 'filt'), may hold values from -0.125 to 0.125
- biases: float32 [4, 256], P('section', 'filt'), may hold values from -3 to 3
- cotangent: bfloat16 [16, 256, 4, 2, 128], P('groups', 'filt'), parts along dimension 0, may hold values from -6 to 6
Outputs:
- grad_weights: float32 [8, 256, 27, 256], P(('groups', 'section'), 'filt'), parts along dimension 0
- grad_biases: float32 [8, 256], P(('groups', 'section'), 'filt'), parts along dimension 0
- grad_inputs: bfloat16 [8, 8, 256, 4, 2, 128], P(('groups', 'section'), None, 'filt'), parts along dimension 0
There are 2 independent parts, one for each index of `groups`. A program takes and returns all parts, laid end to end along the dimension named above; an argument that names none is the same for every part. Nothing has to cross between parts.
All inputs are finite; a program needn't handle non-finite values.
Results may differ from a plain program's by a relative error of at most 0.019.
Values may be sent and summed in bfloat16 or wider, within the bound.
No kernel may reach another device: no remote copies, remote signals or barrier semaphores. Data moves between devices by JAX's collectives and lax.ppermute only.
A program may use at most 64 MiB of HBM per device.

v0:
```python
import math
import jax
import jax.numpy as jnp
from jax import lax
from jax.sharding import PartitionSpec as P

CHUNK = 1
PAD3 = ((1, 1), (1, 1), (1, 1))


def silu_slope(pre_act):
    sigmoid = jax.nn.sigmoid(pre_act)
    return sigmoid * (1.0 + pre_act * (1.0 - sigmoid))


def conv_forward(act, kernel):
    return lax.conv_general_dilated(
        act,
        kernel,
        (1, 1, 1),
        PAD3,
        dimension_numbers=("NCDHW", "ODHWI", "NCDHW"),
        preferred_element_type=jnp.float32,
    )


def conv_input_grad(slope, kernel):
    flipped = kernel[:, ::-1, ::-1, ::-1, :]
    return lax.conv_general_dilated(
        slope,
        flipped,
        (1, 1, 1),
        PAD3,
        dimension_numbers=("NCDHW", "IDHWO", "NCDHW"),
        preferred_element_type=jnp.float32,
    )


def conv_weight_grad(act, slope):
    return lax.conv_general_dilated(
        act,
        slope,
        (1, 1, 1),
        PAD3,
        dimension_numbers=("CNDHW", "IODHW", "CDHWN"),
        preferred_element_type=jnp.float32,
    )


def local(volumes, weights, biases, cotangent):
    section_count = lax.axis_size("section")
    section_pos = lax.axis_index("section")
    micro_count = volumes.shape[0]
    chunk = CHUNK if micro_count % CHUNK == 0 else 1
    chunk_count = micro_count // chunk
    tick_count = chunk_count + section_count - 1
    own_count, tap_count, channels = weights.shape[1:]
    extent = volumes.shape[2:]
    kernel = weights[0].reshape(own_count, 3, 3, 3, channels)
    layer_bias = biases[0][None, :, None, None, None]
    slab = (chunk, own_count) + tuple(extent)
    forward_pairs = [(i, i + 1) for i in range(section_count - 1)]
    backward_pairs = [(i + 1, i) for i in range(section_count - 1)]
    incoming = jnp.zeros(slab, jnp.bfloat16)
    gathered = []
    pres = []
    for tick in range(tick_count):
        if tick < chunk_count:
            first = volumes[tick * chunk : (tick + 1) * chunk]
        else:
            first = jnp.zeros(slab, jnp.bfloat16)
        own_input = jnp.where(section_pos == 0, first, incoming)
        full_input = lax.all_gather(own_input, "filt", axis=1, tiled=True)
        pre_act = conv_forward(full_input, kernel) + layer_bias
        gathered.append(full_input)
        pres.append(pre_act)
        if tick < tick_count - 1:
            outgoing = jax.nn.silu(pre_act).astype(jnp.bfloat16)
            incoming = lax.ppermute(outgoing, "section", forward_pairs)
    incoming = jnp.zeros(slab, jnp.bfloat16)
    grad_kernel = jnp.zeros((own_count, 3, 3, 3, channels), jnp.float32)
    grad_bias = jnp.zeros((own_count,), jnp.float32)
    results = []
    for tick in range(tick_count):
        forward_tick = tick_count - 1 - tick
        if tick < chunk_count:
            start = (chunk_count - 1 - tick) * chunk
            last = cotangent[start : start + chunk]
        else:
            last = jnp.zeros(slab, jnp.bfloat16)
        upstream = jnp.where(section_pos == section_count - 1, last, incoming)
        sample = forward_tick - section_pos
        in_range = (sample >= 0) & (sample < chunk_count)
        slope = (upstream.astype(jnp.float32) * silu_slope(pres[forward_tick])).astype(jnp.bfloat16)
        slope = jnp.where(in_range, slope, jnp.zeros((), jnp.bfloat16))
        grad_kernel = grad_kernel + conv_weight_grad(gathered[forward_tick], slope)
        grad_bias = grad_bias + jnp.sum(slope.astype(jnp.float32), axis=(0, 2, 3, 4))
        partial = jnp.moveaxis(conv_input_grad(slope, kernel).astype(jnp.bfloat16), 1, 0)
        partial = partial.reshape(channels, chunk * extent[0] * extent[1], extent[2])
        scattered = lax.psum_scatter(partial, "filt", scatter_dimension=0, tiled=True)
        input_grad = jnp.moveaxis(scattered.reshape((own_count, chunk) + tuple(extent)), 0, 1)
        results.append(input_grad)
        if tick < tick_count - 1:
            incoming = lax.ppermute(input_grad, "section", backward_pairs)
    reversed_results = jnp.stack(results[::-1])
    picked = lax.dynamic_slice_in_dim(reversed_results, section_pos, chunk_count, axis=0)
    grad_in = picked.reshape((1, micro_count, own_count) + tuple(extent))
    norm_scale = 1.0 / math.sqrt(micro_count * math.prod(extent))
    return (
        (grad_kernel * norm_scale).reshape(1, own_count, tap_count, channels),
        (grad_bias * norm_scale)[None],
        grad_in,
    )


def solution(mesh):
    in_specs = (
        P("groups", "filt", None, None, None),
        P("section", "filt", None, None),
        P("section", "filt"),
        P("groups", "filt", None, None, None),
    )
    out_specs = (
        P(("groups", "section"), "filt", None, None),
        P(("groups", "section"), "filt"),
        P(("groups", "section"), None, "filt", None, None, None),
    )
    return jax.shard_map(local, mesh=mesh, in_specs=in_specs, out_specs=out_specs, check_vma=False)
```

profile of v0, /device:TPU:1, one launch (start us, length us, event | category | flops | bytes accessed | tf_op | source)
XLA Modules:
  0.0 906.7 jit_solution(9746588383378449853)
XLA Ops:
  10.6 15.3 %all_gather.33 = bf16[1,256,4,2,128]{4,2,3,0,1:T(4,128)(2,1)S(1)} all-gather(bf16[1,64,4,2,128]{4,2,3,0,1:T(4,128)(2,1)S(1)} %copy.410), channel_id=1, replica_groups=mesh['groups'=2,'section'=4,'filt'=4] {'filt'}, dimensions={1}, use_global_device_ids=true | all-gather | bytes 655360 | tf_op jit(solution)/shard_map/all_gather | solution.py:73
  71.6 13.6 %all_gather.35 = bf16[1,256,4,2,128]{4,2,3,0,1:T(4,128)(2,1)S(1)} all-gather(bf16[1,64,4,2,128]{4,2,3,0,1:T(4,128)(2,1)S(1)} %copy.422), channel_id=1, replica_groups=mesh['groups'=2,'section'=4,'filt'=4] {'filt'}, dimensions={1}, use_global_device_ids=true | all-gather | bytes 655360 | tf_op jit(solution)/shard_map/all_gather | solution.py:73
  101.7 13.5 %all_gather.36 = bf16[1,256,4,2,128]{4,2,3,0,1:T(4,128)(2,1)S(1)} all-gather(bf16[1,64,4,2,128]{4,2,3,0,1:T(4,128)(2,1)S(1)} %copy.428), channel_id=1, replica_groups=mesh['groups'=2,'section'=4,'filt'=4] {'filt'}, dimensions={1}, use_global_device_ids=true | all-gather | bytes 655360 | tf_op jit(solution)/shard_map/all_gather | solution.py:73
  136.2 13.4 %all_gather.37 = bf16[1,256,4,2,128]{4,2,3,0,1:T(4,128)(2,1)S(1)} all-gather(bf16[1,64,4,2,128]{4,2,3,0,1:T(4,128)(2,1)} %copy.434), channel_id=1, replica_groups=mesh['groups'=2,'section'=4,'filt'=4] {'filt'}, dimensions={1}, use_global_device_ids=true | all-gather | bytes 655360 | tf_op jit(solution)/shard_map/all_gather | solution.py:73
  174.5 14.0 %all_gather.38 = bf16[1,256,4,2,128]{4,2,3,0,1:T(4,128)(2,1)S(1)} all-gather(bf16[1,64,4,2,128]{4,2,3,0,1:T(4,128)(2,1)} %copy.440), channel_id=1, replica_groups=mesh['groups'=2,'section'=4,'filt'=4] {'filt'}, dimensions={1}, use_global_device_ids=true | all-gather | bytes 655360 | tf_op jit(solution)/shard_map/all_gather | solution.py:73
  213.3 13.6 %all_gather.39 = bf16[1,256,4,2,128]{4,2,3,0,1:T(4,128)(2,1)S(1)} all-gather(bf16[1,64,4,2,128]{4,2,3,0,1:T(4,128)(2,1)} %copy.446), channel_id=1, replica_groups=mesh['groups'=2,'section'=4,'filt'=4] {'filt'}, dimensions={1}, use_global_device_ids=true | all-gather | bytes 655360 | tf_op jit(solution)/shard_map/all_gather | solution.py:73
  251.9 13.9 %all_gather.40 = bf16[1,256,4,2,128]{4,2,3,0,1:T(4,128)(2,1)S(1)} all-gather(bf16[1,64,4,2,128]{4,2,3,0,1:T(4,128)(2,1)} %copy.452), channel_id=1, replica_groups=mesh['groups'=2,'section'=4,'filt'=4] {'filt'}, dimensions={1}, use_global_device_ids=true | all-gather | bytes 655360 | tf_op jit(solution)/shard_map/all_gather | solution.py:73
  366.4 13.3 %all_gather.43 = bf16[1,256,4,2,128]{4,2,3,0,1:T(4,128)(2,1)S(1)} all-gather(bf16[1,64,4,2,128]{4,2,3,0,1:T(4,128)(2,1)} %copy.470), channel_id=1, replica_groups=mesh['groups'=2,'section'=4,'filt'=4] {'filt'}, dimensions={1}, use_global_device_ids=true | all-gather | bytes 655360 | tf_op jit(solution)/shard_map/all_gather | solution.py:73
  401.5 24.4 %reduce-scatter.12.cloned.1.call-done = bf16[64,8,128]{2,0,1:T(8,128)(2,1)} async-done(((bf16[256,8,128]{2,0,1:T(8,128)(2,1)}), bf16[64,8,128]{2,0,1:T(8,128)(2,1)}) %reduce-scatter.12.cloned.1.call-update) | async-done | bytes 131088 | tf_op jit(solution)/shard_map/reduce_scatter | solution.py:100
  449.8 17.2 %reduce-scatter.14.cloned.1.call-done = bf16[64,8,128]{2,0,1:T(8,128)(2,1)} async-done(((bf16[256,8,128]{2,0,1:T(8,128)(2,1)}), bf16[64,8,128]{2,0,1:T(8,128)(2,1)}) %reduce-scatter.14.cloned.1.call-update) | async-done | bytes 131088 | tf_op jit(solution)/shard_map/reduce_scatter | solution.py:100
  490.7 17.2 %reduce-scatter.16.cloned.1.call-done = bf16[64,8,128]{2,0,1:T(8,128)(2,1)} async-done(((bf16[256,8,128]{2,0,1:T(8,128)(2,1)}), bf16[64,8,128]{2,0,1:T(8,128)(2,1)}) %reduce-scatter.16.cloned.1.call-update) | async-done | bytes 131088 | tf_op jit(solution)/shard_map/reduce_scatter | solution.py:100
  531.7 17.3 %reduce-scatter.18.cloned.1.call-done = bf16[64,8,128]{2,0,1:T(8,128)(2,1)} async-done(((bf16[256,8,128]{2,0,1:T(8,128)(2,1)}), bf16[64,8,128]{2,0,1:T(8,128)(2,1)}) %reduce-scatter.18.cloned.1.call-update) | async-done | bytes 131088 | tf_op jit(solution)/shard_map/reduce_scatter | solution.py:100
  572.3 17.2 %reduce-scatter.20.cloned.1.call-done = bf16[64,8,128]{2,0,1:T(8,128)(2,1)} async-done(((bf16[256,8,128]{2,0,1:T(8,128)(2,1)}), bf16[64,8,128]{2,0,1:T(8,128)(2,1)}) %reduce-scatter.20.cloned.1.call-update) | async-done | bytes 131088 | tf_op jit(solution)/shard_map/reduce_scatter | solution.py:100
  652.1 17.7 %fusion.153 = f32[64,3,3,3,256]{4,0,3,2,1:T(8,128)} fusion(bf16[1,256,4,2,128]{1,0,4,3,2:T(2,128)(2,1)} %copy.477, bf16[1,64,4,2,128]{1,3,4,2,0:T(2,128)(2,1)S(1)} %copy-done.17), kind=kOutput, calls=%fused_computation.241 | convolution fusion | flops 500695040 | bytes 2424832 | tf_op jit(solution)/shard_map/conv_general_dilated | solution.py:40
  674.9 16.8 %fusion.151 = f32[64,3,3,3,256]{4,0,3,2,1:T(8,128)} fusion(bf16[1,256,4,2,128]{1,0,4,3,2:T(2,128)(2,1)S(1)} %copy-done.26, bf16[1,64,4,2,128]{1,3,4,2,0:T(2,128)(2,1)S(1)} %copy-done.28), kind=kOutput, calls=%fused_computation.239 | convolution fusion | flops 500695040 | bytes 2424832 | tf_op jit(solution)/shard_map/conv_general_dilated | solution.py:40
  698.9 16.5 %fusion.149 = f32[64,3,3,3,256]{4,0,3,2,1:T(8,128)} fusion(bf16[1,256,4,2,128]{1,0,4,3,2:T(2,128)(2,1)S(1)} %copy-done.25, bf16[1,64,4,2,128]{1,3,4,2,0:T(2,128)(2,1)S(1)} %copy-done.29), kind=kOutput, calls=%fused_computation.237 | convolution fusion | flops 500695040 | bytes 2424832 | tf_op jit(solution)/shard_map/conv_general_dilated | solution.py:40
  720.6 16.8 %fusion.147 = f32[64,3,3,3,256]{4,0,3,2,1:T(8,128)} fusion(bf16[1,256,4,2,128]{1,0,4,3,2:T(2,128)(2,1)S(1)} %copy-done.24, bf16[1,64,4,2,128]{1,3,4,2,0:T(2,128)(2,1)S(1)} %copy-done.30), kind=kOutput, calls=%fused_computation.235 | convolution fusion | flops 500695040 | bytes 2424832 | tf_op jit(solution)/shard_map/conv_general_dilated | solution.py:40
  744.1 16.6 %fusion.145 = f32[64,3,3,3,256]{4,0,3,2,1:T(8,128)} fusion(bf16[1,256,4,2,128]{1,0,4,3,2:T(2,128)(2,1)S(1)} %copy-done.23, bf16[1,64,4,2,128]{1,3,4,2,0:T(2,128)(2,1)S(1)} %copy-done.31), kind=kOutput, calls=%fused_computation.233 | convolution fusion | flops 500695040 | bytes 2424832 | tf_op jit(solution)/shard_map/conv_general_dilated | solution.py:40
  765.1 18.0 %fusion.143 = f32[64,3,3,3,256]{4,0,3,2,1:T(8,128)} fusion(bf16[1,256,4,2,128]{1,0,4,3,2:T(2,128)(2,1)} %copy.532, bf16[1,64,4,2,128]{1,3,4,2,0:T(2,128)(2,1)S(1)} %copy-done.32), kind=kOutput, calls=%fused_computation.231 | convolution fusion | flops 500695040 | bytes 2424832 | tf_op jit(solution)/shard_map/conv_general_dilated | solution.py:40
  788.7 16.6 %fusion.141 = f32[64,3,3,3,256]{4,0,3,2,1:T(8,128)} fusion(bf16[1,256,4,2,128]{1,0,4,3,2:T(2,128)(2,1)S(1)} %copy-done.22, bf16[1,64,4,2,128]{1,3,4,2,0:T(2,128)(2,1)S(1)} %copy-done.34), kind=kOutput, calls=%fused_computation.229 | convolution fusion | flops 500695040 | bytes 2424832 | tf_op jit(solution)/shard_map/conv_general_dilated | solution.py:40
  809.7 18.0 %fusion.139 = f32[64,3,3,3,256]{4,0,3,2,1:T(8,128)} fusion(bf16[1,256,4,2,128]{1,0,4,3,2:T(2,128)(2,1)} %copy.554, bf16[1,64,4,2,128]{1,3,4,2,0:T(2,128)(2,1)S(1)} %copy-done.36), kind=kOutput, calls=%fused_computation.227 | convolution fusion | flops 500695040 | bytes 2424832 | tf_op jit(solution)/shard_map/conv_general_dilated | solution.py:40
  833.2 16.5 %fusion.137 = f32[64,3,3,3,256]{4,0,3,2,1:T(8,128)} fusion(bf16[1,256,4,2,128]{1,0,4,3,2:T(2,128)(2,1)S(1)} %copy-done.21, bf16[1,64,4,2,128]{1,3,4,2,0:T(2,128)(2,1)S(1)} %get-tuple-element.20), kind=kOutput, calls=%fused_computation.225 | convolution fusion | flops 500695040 | bytes 2424832 | tf_op jit(solution)/shard_map/conv_general_dilated | solution.py:40
  854.1 16.7 %fusion.134 = f32[64,3,3,3,256]{4,0,3,2,1:T(8,128)} fusion(bf16[1,256,4,2,128]{1,0,4,3,2:T(2,128)(2,1)S(1)} %copy-done.19, bf16[1,64,4,2,128]{1,3,4,2,0:T(2,128)(2,1)S(1)} %get-tuple-element.24), kind=kOutput, calls=%fused_computation.222 | convolution fusion | flops 500695040 | bytes 2424832 | tf_op jit(solution)/shard_map/conv_general_dilated | solution.py:40
  870.9 24.5 %add_multiply_fusion = f32[64,3,3,3,256]{4,0,3,2,1:T(8,128)} fusion(f32[64,3,3,3,256]{4,0,3,2,1:T(8,128)} %fusion.134, f32[64,3,3,3,256]{4,0,3,2,1:T(8,128)} %fusion.137, f32[64,3,3,3,256]{4,0,3,2,1:T(8,128)} %fusion.139, f32[64,3,3,3,256]{4,0,3,2,1:T(8,128)} %fusion.141, f32[64,3,3,3,256]{4,0,3,2,1:T(8,128)} %fusion.143, f32[64,3,3,3,256]{4,0,3,2,1:T(8,128)} %fusion.145, ...), kind=kOutput, calls=%fused_computation | convolution fusion | flops 505561088 | bytes 20119552 | tf_op jit(solution)/shard_map/conv_general_dilated | solution.py:40
  (481 shorter events, 492.0 us)
Async XLA Ops:
  7.2 418.7 %reduce-scatter.12.cloned.1.call-start = ((), (), s32[]{:S(2)}) async-start(), calls=%async_computation.11 | async-start | bytes 655360 | tf_op jit(solution)/shard_map/reduce_scatter | solution.py:100
  60.8 10.6 %collective-permute-start.1 = (bf16[1,64,4,2,128]{1,3,4,2,0:T(2,128)(2,1)S(1)}, bf16[1,64,4,2,128]{1,3,4,2,0:T(2,128)(2,1)S(1)}, u32[]{:S(2)}, u32[]{:S(2)}) collective-permute-start(bf16[1,64,4,2,128]{1,3,4,2,0:T(2,128)(2,1)S(1)} %slice_bitcast_fusion.30), channel_id=1, source_target_pairs={{0,4},{4,8},{8,12},{1,5},{5,9},{9,13},{2,6},{6,10},{10,14},{3,7},{... | collective-permute-start | bytes 393224 | tf_op jit(solution)/shard_map/ppermute | solution.py:79
  91.6 9.9 %collective-permute-start.2 = (bf16[1,64,4,2,128]{1,3,4,2,0:T(2,128)(2,1)S(1)}, bf16[1,64,4,2,128]{1,3,4,2,0:T(2,128)(2,1)S(1)}, u32[]{:S(2)}, u32[]{:S(2)}) collective-permute-start(bf16[1,64,4,2,128]{1,3,4,2,0:T(2,128)(2,1)S(1)} %slice_bitcast_fusion.29), channel_id=1, source_target_pairs={{0,4},{4,8},{8,12},{1,5},{5,9},{9,13},{2,6},{6,10},{10,14},{3,7},{... | collective-permute-start | bytes 393224 | tf_op jit(solution)/shard_map/ppermute | solution.py:79
  124.0 10.4 %collective-permute-start.3 = (bf16[1,64,4,2,128]{1,3,4,2,0:T(2,128)(2,1)}, bf16[1,64,4,2,128]{1,3,4,2,0:T(2,128)(2,1)}, u32[]{:S(2)}, u32[]{:S(2)}) collective-permute-start(bf16[1,64,4,2,128]{1,3,4,2,0:T(2,128)(2,1)} %slice_bitcast_fusion.28), channel_id=1, source_target_pairs={{0,4},{4,8},{8,12},{1,5},{5,9},{9,13},{2,6},{6,10},{10,14},{3,7},{... | collective-permute-start | bytes 393224 | tf_op jit(solution)/shard_map/ppermute | solution.py:79
  160.2 10.8 %collective-permute-start.4 = (bf16[1,64,4,2,128]{1,3,4,2,0:T(2,128)(2,1)}, bf16[1,64,4,2,128]{1,3,4,2,0:T(2,128)(2,1)}, u32[]{:S(2)}, u32[]{:S(2)}) collective-permute-start(bf16[1,64,4,2,128]{1,3,4,2,0:T(2,128)(2,1)} %slice_bitcast_fusion.27), channel_id=1, source_target_pairs={{0,4},{4,8},{8,12},{1,5},{5,9},{9,13},{2,6},{6,10},{10,14},{3,7},{... | collective-permute-start | bytes 393224 | tf_op jit(solution)/shard_map/ppermute | solution.py:79
  199.8 10.0 %collective-permute-start.5 = (bf16[1,64,4,2,128]{1,3,4,2,0:T(2,128)(2,1)}, bf16[1,64,4,2,128]{1,3,4,2,0:T(2,128)(2,1)}, u32[]{:S(2)}, u32[]{:S(2)}) collective-permute-start(bf16[1,64,4,2,128]{1,3,4,2,0:T(2,128)(2,1)} %slice_bitcast_fusion.26), channel_id=1, source_target_pairs={{0,4},{4,8},{8,12},{1,5},{5,9},{9,13},{2,6},{6,10},{10,14},{3,7},{... | collective-permute-start | bytes 393224 | tf_op jit(solution)/shard_map/ppermute | solution.py:79
  238.1 10.3 %collective-permute-start.6 = (bf16[1,64,4,2,128]{1,3,4,2,0:T(2,128)(2,1)}, bf16[1,64,4,2,128]{1,3,4,2,0:T(2,128)(2,1)}, u32[]{:S(2)}, u32[]{:S(2)}) collective-permute-start(bf16[1,64,4,2,128]{1,3,4,2,0:T(2,128)(2,1)} %slice_bitcast_fusion.25), channel_id=1, source_target_pairs={{0,4},{4,8},{8,12},{1,5},{5,9},{9,13},{2,6},{6,10},{10,14},{3,7},{... | collective-permute-start | bytes 393224 | tf_op jit(solution)/shard_map/ppermute | solution.py:79
  313.5 10.8 %collective-permute-start.8 = (bf16[1,64,4,2,128]{1,3,4,2,0:T(2,128)(2,1)}, bf16[1,64,4,2,128]{1,3,4,2,0:T(2,128)(2,1)}, u32[]{:S(2)}, u32[]{:S(2)}) collective-permute-start(bf16[1,64,4,2,128]{1,3,4,2,0:T(2,128)(2,1)} %slice_bitcast_fusion.23), channel_id=1, source_target_pairs={{0,4},{4,8},{8,12},{1,5},{5,9},{9,13},{2,6},{6,10},{10,14},{3,7},{... | collective-permute-start | bytes 393224 | tf_op jit(solution)/shard_map/ppermute | solution.py:79
  352.3 10.4 %collective-permute-start.9 = (bf16[1,64,4,2,128]{1,3,4,2,0:T(2,128)(2,1)}, bf16[1,64,4,2,128]{1,3,4,2,0:T(2,128)(2,1)}, u32[]{:S(2)}, u32[]{:S(2)}) collective-permute-start(bf16[1,64,4,2,128]{1,3,4,2,0:T(2,128)(2,1)} %slice_bitcast_fusion.22), channel_id=1, source_target_pairs={{0,4},{4,8},{8,12},{1,5},{5,9},{9,13},{2,6},{6,10},{10,14},{3,7},{... | collective-permute-start | bytes 393224 | tf_op jit(solution)/shard_map/ppermute | solution.py:79
  401.5 65.5 %reduce-scatter.14.cloned.1.call-start = ((), (), s32[]{:S(2)}) async-start(), calls=%async_computation.12 | async-start | bytes 655360 | tf_op jit(solution)/shard_map/reduce_scatter | solution.py:100
  449.7 58.2 %reduce-scatter.16.cloned.1.call-start = ((), (), s32[]{:S(2)}) async-start(), calls=%async_computation.13 | async-start | bytes 655360 | tf_op jit(solution)/shard_map/reduce_scatter | solution.py:100
  490.7 58.3 %reduce-scatter.18.cloned.1.call-start = ((), (), s32[]{:S(2)}) async-start(), calls=%async_computation.14 | async-start | bytes 655360 | tf_op jit(solution)/shard_map/reduce_scatter | solution.py:100
  531.7 57.9 %reduce-scatter.20.cloned.1.call-start = ((), (), s32[]{:S(2)}) async-start(), calls=%async_computation.15 | async-start | bytes 655360 | tf_op jit(solution)/shard_map/reduce_scatter | solution.py:100
  572.3 76.2 %reduce-scatter.22.cloned.1.call-start = ((), (), s32[]{:S(2)}) async-start(), calls=%async_computation.16 | async-start | bytes 655360 | tf_op jit(solution)/shard_map/reduce_scatter | solution.py:100
  612.8 80.7 %reduce-scatter.24.cloned.1.call-start = ((), (), s32[]{:S(2)}) async-start(), calls=%async_computation.17 | async-start | bytes 655360 | tf_op jit(solution)/shard_map/reduce_scatter | solution.py:100
  649.6 20.3 %collective-permute-start.15 = (bf16[1,64,4,2,128]{1,3,4,2,0:T(2,128)(2,1)S(1)}, bf16[1,64,4,2,128]{1,3,4,2,0:T(2,128)(2,1)S(1)}, u32[]{:S(2)}, u32[]{:S(2)}) collective-permute-start(bf16[1,64,4,2,128]{1,3,4,2,0:T(2,128)(2,1)S(1)} %copy.541), channel_id=1, source_target_pairs={{4,0},{8,4},{12,8},{5,1},{9,5},{13,9},{6,2},{10,6},{14,10},{7,3},{... | collective-permute-start | bytes 393224 | tf_op jit(solution)/shard_map/ppermute | solution.py:104
  674.9 63.8 %reduce-scatter.26.cloned.1.call-start = ((), (), s32[]{:S(2)}) async-start(), calls=%async_computation.18 | async-start | bytes 655360 | tf_op jit(solution)/shard_map/reduce_scatter | solution.py:100
  694.6 20.9 %collective-permute-start.16 = (bf16[1,64,4,2,128]{1,3,4,2,0:T(2,128)(2,1)S(1)}, bf16[1,64,4,2,128]{1,3,4,2,0:T(2,128)(2,1)S(1)}, u32[]{:S(2)}, u32[]{:S(2)}) collective-permute-start(bf16[1,64,4,2,128]{1,3,4,2,0:T(2,128)(2,1)S(1)} %copy.552), channel_id=1, source_target_pairs={{4,0},{8,4},{12,8},{5,1},{9,5},{13,9},{6,2},{10,6},{14,10},{7,3},{... | collective-permute-start | bytes 393224 | tf_op jit(solution)/shard_map/ppermute | solution.py:104
  720.5 62.7 %reduce-scatter.28.cloned.1.call-start = ((), (), s32[]{:S(2)}) async-start(), calls=%async_computation.19 | async-start | bytes 655360 | tf_op jit(solution)/shard_map/reduce_scatter | solution.py:100
  739.7 21.0 %collective-permute-start.17 = (bf16[1,64,4,2,128]{1,3,4,2,0:T(2,128)(2,1)S(1)}, bf16[1,64,4,2,128]{1,3,4,2,0:T(2,128)(2,1)S(1)}, u32[]{:S(2)}, u32[]{:S(2)}) collective-permute-start(bf16[1,64,4,2,128]{1,3,4,2,0:T(2,128)(2,1)S(1)} %copy.562), channel_id=1, source_target_pairs={{4,0},{8,4},{12,8},{5,1},{9,5},{13,9},{6,2},{10,6},{14,10},{7,3},{... | collective-permute-start | bytes 393224 | tf_op jit(solution)/shard_map/ppermute | solution.py:104
  765.1 62.7 %reduce-scatter.30.cloned.1.call-start = ((), (), s32[]{:S(2)}) async-start(), calls=%async_computation.20 | async-start | bytes 655360 | tf_op jit(solution)/shard_map/reduce_scatter | solution.py:100
  784.2 21.0 %collective-permute-start.18 = (bf16[1,64,4,2,128]{1,3,4,2,0:T(2,128)(2,1)S(1)}, bf16[1,64,4,2,128]{1,3,4,2,0:T(2,128)(2,1)S(1)}, u32[]{:S(2)}, u32[]{:S(2)}) collective-permute-start(bf16[1,64,4,2,128]{1,3,4,2,0:T(2,128)(2,1)S(1)} %copy.572), channel_id=1, source_target_pairs={{4,0},{8,4},{12,8},{5,1},{9,5},{13,9},{6,2},{10,6},{14,10},{7,3},{... | collective-permute-start | bytes 393224 | tf_op jit(solution)/shard_map/ppermute | solution.py:104
  809.7 86.4 %reduce-scatter.32.cloned.1.call-start = ((), (), s32[]{:S(2)}) async-start(), calls=%async_computation.21 | async-start | bytes 655360 | tf_op jit(solution)/shard_map/reduce_scatter | solution.py:100
  828.8 20.9 %collective-permute-start.19 = (bf16[1,64,4,2,128]{1,3,4,2,0:T(2,128)(2,1)S(1)}, bf16[1,64,4,2,128]{1,3,4,2,0:T(2,128)(2,1)S(1)}, u32[]{:S(2)}, u32[]{:S(2)}) collective-permute-start(bf16[1,64,4,2,128]{1,3,4,2,0:T(2,128)(2,1)S(1)} %copy.582), channel_id=1, source_target_pairs={{4,0},{8,4},{12,8},{5,1},{9,5},{13,9},{6,2},{10,6},{14,10},{7,3},{... | collective-permute-start | bytes 393224 | tf_op jit(solution)/shard_map/ppermute | solution.py:104
  (71 other events, 712.7 us)
Sparse Core Ops, SparseCore 0:
  401.6 24.2 reduce-scatter.11
  449.8 17.0 reduce-scatter.13
  490.8 17.0 reduce-scatter.15
  531.8 17.1 reduce-scatter.17
  572.4 17.1 reduce-scatter.19
  612.9 17.0 reduce-scatter.21
  675.0 18.4 reduce-scatter.23
  720.6 17.9 reduce-scatter.25
  765.2 17.9 reduce-scatter.27
  809.8 17.8 reduce-scatter.29
  854.2 17.8 reduce-scatter.31
where the time goes:
time: 918 us; the launch traced here: 907 us
  matrix products  261 us (28%)
  local copies, waits for them, and re-layouts  210 us (23%)
  blocking collectives  150 us (16%)
  waiting for transfers between devices  131 us (14%)
  starting transfers between devices  109 us (12%)
  other arithmetic  29.2 us (3%)
  between operations  16 us (2%)
    conv_general_dilated x11, matrix products, conv_weight_grad(): lax.conv_general_dilated(act, slope, (1, 1, 1), PAD3, dimension_numbers=(...  195 us
    all_gather x11, blocking collectives, local(): full_input = lax.all_gather(own_input, 'filt', axis=1, tiled=True)  150 us
    reduce_scatter x11, waiting for transfers between devices, local(): lax.psum_scatter(partial, 'filt', scatter_dimension=0, tiled=True)  96.3 us
    ppermute x10, starting transfers between devices, local(): incoming = lax.ppermute(outgoing, 'section', forward_pairs)  66.7 us
    unnamed x176, local copies, waits for them, and re-layouts  58.6 us
    conv_general_dilated x11, matrix products, conv_forward(): lax.conv_general_dilated(act, kernel, (1, 1, 1), PAD3, dimension_numbers=...  52.9 us
    all_gather x33, local copies, waits for them, and re-layouts, local(): full_input = lax.all_gather(own_input, 'filt', axis=1, tiled=True)  43 us
    ppermute x10, starting transfers between devices, local(): incoming = lax.ppermute(input_grad, 'section', backward_pairs)  41.7 us
  transfers between devices with their start and end apart: 31, of which 22 were waited for; matrix products, arithmetic and copies ran while one was open for 28% of the time, Pallas kernels for 0%

commit v1 on v0

--- a/solution.py
+++ b/solution.py
@@ -3,6 +3,7 @@
 import jax.numpy as jnp
 from jax import lax
 from jax.sharding import PartitionSpec as P
+from jax.lax import axis_index, axis_size, ppermute
 
 CHUNK = 1
 PAD3 = ((1, 1), (1, 1), (1, 1))
@@ -70,7 +71,38 @@
         else:
             first = jnp.zeros(slab, jnp.bfloat16)
         own_input = jnp.where(section_pos == 0, first, incoming)
-        full_input = lax.all_gather(own_input, "filt", axis=1, tiled=True)
+
+        def rest_lanes_all(out_dim, point):
+            placed = axis_index("filt")
+            k_now = axis_size("filt")
+            reached, piece_out, mixed_arr = (k_now, placed, point.shape[out_dim])
+            pages = [idx * reached if at == out_dim else idx for at, idx in enumerate(point.shape)]
+            q_next = jnp.zeros(pages, point.dtype)
+            y_new = lax.dynamic_update_slice_in_dim(
+                q_next, point, piece_out * mixed_arr, axis=out_dim
+            )
+            e_now = item_now = point
+            for dev in range(1, reached // 2 + 1):
+                e_now = ppermute(
+                    e_now,
+                    axis_name="filt",
+                    perm=[(at, (at + 1) % reached) for at in range(reached)],
+                )
+                y_new = lax.dynamic_update_slice_in_dim(
+                    y_new, e_now, (piece_out - dev) % reached * mixed_arr, axis=out_dim
+                )
+                if 2 * dev < reached:
+                    item_now = ppermute(
+                        item_now,
+                        axis_name="filt",
+                        perm=[(at, (at - 1) % reached) for at in range(reached)],
+                    )
+                    y_new = lax.dynamic_update_slice_in_dim(
+                        y_new, item_now, (piece_out + dev) % reached * mixed_arr, axis=out_dim
+                    )
+            return y_new
+
+        full_input = rest_lanes_all(1, own_input)
         pre_act = conv_forward(full_input, kernel) + layer_bias
         gathered.append(full_input)
         pres.append(pre_act)

time: 918 us -> 770 us (0.84)
  blocking collectives: 150 us -> 0 us
  local copies, waits for them, and re-layouts: 210 us -> 126 us
  waiting for transfers between devices: 131 us -> 192 us
  starting transfers between devices: 109 us -> 146 us
  other arithmetic: 29.2 us -> 15.7 us
    all_gather x11 -> x0, blocking collectives: 150 us -> none  [local(): full_input = lax.all_gather(own_input, 'filt', axis=1, tiled=True)]
    ppermute x0 -> x33, waiting for transfers between devices: none -> 76.6 us  [the longest x22 74.2 us: rest_lanes_all(): ppermute(e_now, axis_name='filt', perm=[(at, (at + 1) % reached) for at i...]
    all_gather x33 -> x0, local copies, waits for them, and re-layouts: 43 us -> none  [local(): full_input = lax.all_gather(own_input, 'filt', axis=1, tiled=True)]
    dynamic_update_slice x0 -> x55, local copies, waits for them, and re-layouts: none -> 41.1 us  [the longest x44 36.2 us: rest_lanes_all(): lax.dynamic_update_slice_in_dim(y_new, e_now, (piece_out - dev) % reached...]
    ppermute x0 -> x33, starting transfers between devices: none -> 38.5 us  [the longest x11 34.7 us: rest_lanes_all(): ppermute(item_now, axis_name='filt', perm=[(at, (at - 1) % reached) for a...]
    unnamed x176 -> x169, local copies, waits for them, and re-layouts: 58.6 us -> 27.6 us
    select_n x11 -> x0, local copies, waits for them, and re-layouts: 12.4 us -> none  [local(): own_input = jnp.where(section_pos == 0, first, incoming)]
    select_n x11 -> x0, other arithmetic: 11 us -> none  [local(): own_input = jnp.where(section_pos == 0, first, incoming)]
  transfers between devices with their start and end apart: 31 -> 64, of which waited for: 22 -> 41; matrix products, arithmetic and copies ran while one was open for 28% -> 34% of each run, Pallas kernels for 0% -> 0%
where the time goes in v1:
time: 770 us; the launch traced here: 760 us
  matrix products  264 us (34%)
  waiting for transfers between devices  192 us (25%)
  starting transfers between devices  146 us (19%)
  local copies, waits for them, and re-layouts  126 us (16%)
  between operations  16.7 us (2%)
  other arithmetic  15.7 us (2%)
    conv_general_dilated x11, matrix products, conv_weight_grad(): lax.conv_general_dilated(act, slope, (1, 1, 1), PAD3, dimension_numbers=(...  198 us
    reduce_scatter x11, waiting for transfers between devices, local(): lax.psum_scatter(partial, 'filt', scatter_dimension=0, tiled=True)  89.8 us
    ppermute x22, waiting for transfers between devices, rest_lanes_all(): ppermute(e_now, axis_name='filt', perm=[(at, (at + 1) % reached) for at i...  74.2 us
    ppermute x10, starting transfers between devices, local(): incoming = lax.ppermute(outgoing, 'section', forward_pairs)  65.8 us
    conv_general_dilated x11, matrix products, conv_forward(): lax.conv_general_dilated(act, kernel, (1, 1, 1), PAD3, dimension_numbers=...  52.9 us
    ppermute x10, starting transfers between devices, local(): incoming = lax.ppermute(input_grad, 'section', backward_pairs)  40.8 us
    dynamic_update_slice x44, local copies, waits for them, and re-layouts, rest_lanes_all(): lax.dynamic_update_slice_in_dim(y_new, e_now, (piece_out - dev) % reached...  36.2 us
    ppermute x11, starting transfers between devices, rest_lanes_all(): ppermute(item_now, axis_name='filt', perm=[(at, (at - 1) % reached) for a...  34.7 us
  transfers between devices with their start and end apart: 64, of which 41 were waited for; matrix products, arithmetic and copies ran while one was open for 34% of the time, Pallas kernels for 0%

profile of v1, /device:TPU:1, one launch (start us, length us, event | category | flops | bytes accessed | tf_op | source)
XLA Modules:
  0.0 760.4 jit_solution(13712565885226044805)
XLA Ops:
  88.2 6.7 collective-permute-start.11
  117.6 6.7 collective-permute-start.15
  147.1 6.7 collective-permute-start.19
  176.6 6.7 collective-permute-start.23
  206.2 6.6 collective-permute-start.27
  235.6 6.7 collective-permute-start.31
  262.4 6.7 collective-permute-start.35
  288.9 6.7 collective-permute-start.39
  321.4 20.9 %reduce-scatter.12.cloned.1.call-done = bf16[64,8,128]{2,0,1:T(8,128)(2,1)} async-done(((bf16[256,8,128]{2,0,1:T(8,128)(2,1)}), bf16[64,8,128]{2,0,1:T(8,128)(2,1)}) %reduce-scatter.12.cloned.1.call-update) | async-done | bytes 131088 | tf_op jit(solution)/shard_map/reduce_scatter | solution.py:132
  355.9 17.2 %reduce-scatter.14.cloned.1.call-done = bf16[64,8,128]{2,0,1:T(8,128)(2,1)} async-done(((bf16[256,8,128]{2,0,1:T(8,128)(2,1)}), bf16[64,8,128]{2,0,1:T(8,128)(2,1)}) %reduce-scatter.14.cloned.1.call-update) | async-done | bytes 131088 | tf_op jit(solution)/shard_map/reduce_scatter | solution.py:132
  386.9 17.2 %reduce-scatter.16.cloned.1.call-done = bf16[64,8,128]{2,0,1:T(8,128)(2,1)} async-done(((bf16[256,8,128]{2,0,1:T(8,128)(2,1)}), bf16[64,8,128]{2,0,1:T(8,128)(2,1)}) %reduce-scatter.16.cloned.1.call-update) | async-done | bytes 131088 | tf_op jit(solution)/shard_map/reduce_scatter | solution.py:132
  417.6 17.3 %reduce-scatter.18.cloned.1.call-done = bf16[64,8,128]{2,0,1:T(8,128)(2,1)} async-done(((bf16[256,8,128]{2,0,1:T(8,128)(2,1)}), bf16[64,8,128]{2,0,1:T(8,128)(2,1)}) %reduce-scatter.18.cloned.1.call-update) | async-done | bytes 131088 | tf_op jit(solution)/shard_map/reduce_scatter | solution.py:132
  448.0 17.1 %reduce-scatter.20.cloned.1.call-done = bf16[64,8,128]{2,0,1:T(8,128)(2,1)} async-done(((bf16[256,8,128]{2,0,1:T(8,128)(2,1)}), bf16[64,8,128]{2,0,1:T(8,128)(2,1)}) %reduce-scatter.20.cloned.1.call-update) | async-done | bytes 131088 | tf_op jit(solution)/shard_map/reduce_scatter | solution.py:132
  507.1 18.0 %fusion.301 = f32[64,3,3,3,256]{4,0,3,2,1:T(8,128)} fusion(bf16[1,256,4,2,128]{1,0,4,3,2:T(2,128)(2,1)S(1)} %copy-done.32, bf16[1,64,4,2,128]{1,0,4,3,2:T(2,128)(2,1)} %copy.294), kind=kOutput, calls=%fused_computation.432 | convolution fusion | flops 500695040 | bytes 2424832 | tf_op jit(solution)/shard_map/conv_general_dilated | solution.py:41
  529.0 16.6 %fusion.302 = f32[64,3,3,3,256]{4,0,3,2,1:T(8,128)} fusion(bf16[1,256,4,2,128]{1,0,4,3,2:T(2,128)(2,1)S(1)} %copy-done.31, bf16[1,64,4,2,128]{1,0,4,3,2:T(2,128)(2,1)S(1)} %copy.304), kind=kOutput, calls=%fused_computation.433 | convolution fusion | flops 500695040 | bytes 2424832 | tf_op jit(solution)/shard_map/conv_general_dilated | solution.py:41
  550.0 18.2 %fusion.303 = f32[64,3,3,3,256]{4,0,3,2,1:T(8,128)} fusion(bf16[1,256,4,2,128]{1,0,4,3,2:T(2,128)(2,1)} %copy.313, bf16[1,64,4,2,128]{1,0,4,3,2:T(2,128)(2,1)S(1)} %copy.314), kind=kOutput, calls=%fused_computation.434 | convolution fusion | flops 500695040 | bytes 2424832 | tf_op jit(solution)/shard_map/conv_general_dilated | solution.py:41
  572.4 16.7 %fusion.304 = f32[64,3,3,3,256]{4,0,3,2,1:T(8,128)} fusion(bf16[1,256,4,2,128]{1,0,4,3,2:T(2,128)(2,1)S(1)} %copy-done.30, bf16[1,64,4,2,128]{1,0,4,3,2:T(2,128)(2,1)S(1)} %copy.324), kind=kOutput, calls=%fused_computation.435 | convolution fusion | flops 500695040 | bytes 2424832 | tf_op jit(solution)/shard_map/conv_general_dilated | solution.py:41
  593.4 18.2 %fusion.305 = f32[64,3,3,3,256]{4,0,3,2,1:T(8,128)} fusion(bf16[1,256,4,2,128]{1,0,4,3,2:T(2,128)(2,1)} %copy.333, bf16[1,64,4,2,128]{1,0,4,3,2:T(2,128)(2,1)S(1)} %copy.334), kind=kOutput, calls=%fused_computation.436 | convolution fusion | flops 500695040 | bytes 2424832 | tf_op jit(solution)/shard_map/conv_general_dilated | solution.py:41
  615.7 16.6 %fusion.306 = f32[64,3,3,3,256]{4,0,3,2,1:T(8,128)} fusion(bf16[1,256,4,2,128]{1,0,4,3,2:T(2,128)(2,1)S(1)} %copy-done.29, bf16[1,64,4,2,128]{1,0,4,3,2:T(2,128)(2,1)S(1)} %copy.344), kind=kOutput, calls=%fused_computation.437 | convolution fusion | flops 500695040 | bytes 2424832 | tf_op jit(solution)/shard_map/conv_general_dilated | solution.py:41
  637.3 18.0 %fusion.307 = f32[64,3,3,3,256]{4,0,3,2,1:T(8,128)} fusion(bf16[1,256,4,2,128]{1,0,4,3,2:T(2,128)(2,1)S(1)} %copy-done.28, bf16[1,64,4,2,128]{1,0,4,3,2:T(2,128)(2,1)} %copy.354), kind=kOutput, calls=%fused_computation.438 | convolution fusion | flops 500695040 | bytes 2424832 | tf_op jit(solution)/shard_map/conv_general_dilated | solution.py:41
  659.6 16.6 %fusion.308 = f32[64,3,3,3,256]{4,0,3,2,1:T(8,128)} fusion(bf16[1,256,4,2,128]{1,0,4,3,2:T(2,128)(2,1)S(1)} %copy-done.27, bf16[1,64,4,2,128]{1,0,4,3,2:T(2,128)(2,1)S(1)} %copy.364), kind=kOutput, calls=%fused_computation.439 | convolution fusion | flops 500695040 | bytes 2424832 | tf_op jit(solution)/shard_map/conv_general_dilated | solution.py:41
  681.2 17.9 %fusion.309 = f32[64,3,3,3,256]{4,0,3,2,1:T(8,128)} fusion(bf16[1,256,4,2,128]{1,0,4,3,2:T(2,128)(2,1)S(1)} %copy-done.26, bf16[1,64,4,2,128]{1,0,4,3,2:T(2,128)(2,1)} %copy.373), kind=kOutput, calls=%fused_computation.440 | convolution fusion | flops 500695040 | bytes 2424832 | tf_op jit(solution)/shard_map/conv_general_dilated | solution.py:41
  703.7 16.6 %fusion.310 = f32[64,3,3,3,256]{4,0,3,2,1:T(8,128)} fusion(bf16[1,256,4,2,128]{1,0,4,3,2:T(2,128)(2,1)S(1)} %copy-done.25, bf16[1,64,4,2,128]{1,0,4,3,2:T(2,128)(2,1)S(1)} %copy.382), kind=kOutput, calls=%fused_computation.441 | convolution fusion | flops 500695040 | bytes 2424832 | tf_op jit(solution)/shard_map/conv_general_dilated | solution.py:41
  724.6 24.3 %add_multiply_fusion = f32[64,3,3,3,256]{4,0,3,2,1:T(8,128)} fusion(f32[64,3,3,3,256]{4,0,3,2,1:T(8,128)} %fusion.310, f32[64,3,3,3,256]{4,0,3,2,1:T(8,128)} %fusion.309, f32[64,3,3,3,256]{4,0,3,2,1:T(8,128)} %fusion.308, f32[64,3,3,3,256]{4,0,3,2,1:T(8,128)} %fusion.307, f32[64,3,3,3,256]{4,0,3,2,1:T(8,128)} %fusion.306, f32[64,3,3,3,256]{4,0,3,2,1:T(8,128)} %fusion.305, ...), kind=kOutput, calls=%fused_computation | convolution fusion | flops 505561088 | bytes 20119552 | tf_op jit(solution)/shard_map/conv_general_dilated | solution.py:41
  (552 shorter events, 403.0 us)
Async XLA Ops:
  7.2 335.1 %reduce-scatter.12.cloned.1.call-start = ((), (), s32[]{:S(2)}) async-start(), calls=%async_computation.11 | async-start | bytes 655360 | tf_op jit(solution)/shard_map/reduce_scatter | solution.py:132
  88.2 8.6 %collective-permute-start.11 = (bf16[1,64,4,2,128]{4,1,3,2,0:T(8,128)(2,1)S(1)}, bf16[1,64,4,2,128]{4,1,3,2,0:T(8,128)(2,1)S(1)}, u32[]{:S(2)}, u32[]{:S(2)}) collective-permute-start(bf16[1,64,4,2,128]{4,1,3,2,0:T(8,128)(2,1)S(1)} %bitcast.469), channel_id=1, source_target_pairs={{0,4},{4,8},{8,12},{1,5},{5,9},{9,13},{2,6},{6,10},{10,14},{3,7},{... | collective-permute-start | bytes 393224 | tf_op jit(solution)/shard_map/ppermute | solution.py:111
  117.6 8.6 %collective-permute-start.15 = (bf16[1,64,4,2,128]{4,1,3,2,0:T(8,128)(2,1)S(1)}, bf16[1,64,4,2,128]{4,1,3,2,0:T(8,128)(2,1)S(1)}, u32[]{:S(2)}, u32[]{:S(2)}) collective-permute-start(bf16[1,64,4,2,128]{4,1,3,2,0:T(8,128)(2,1)S(1)} %bitcast.470), channel_id=1, source_target_pairs={{0,4},{4,8},{8,12},{1,5},{5,9},{9,13},{2,6},{6,10},{10,14},{3,7},{... | collective-permute-start | bytes 393224 | tf_op jit(solution)/shard_map/ppermute | solution.py:111
  147.1 8.6 %collective-permute-start.19 = (bf16[1,64,4,2,128]{4,1,3,2,0:T(8,128)(2,1)S(1)}, bf16[1,64,4,2,128]{4,1,3,2,0:T(8,128)(2,1)S(1)}, u32[]{:S(2)}, u32[]{:S(2)}) collective-permute-start(bf16[1,64,4,2,128]{4,1,3,2,0:T(8,128)(2,1)S(1)} %bitcast.471), channel_id=1, source_target_pairs={{0,4},{4,8},{8,12},{1,5},{5,9},{9,13},{2,6},{6,10},{10,14},{3,7},{... | collective-permute-start | bytes 393224 | tf_op jit(solution)/shard_map/ppermute | solution.py:111
  176.6 8.6 %collective-permute-start.23 = (bf16[1,64,4,2,128]{4,1,3,2,0:T(8,128)(2,1)S(1)}, bf16[1,64,4,2,128]{4,1,3,2,0:T(8,128)(2,1)S(1)}, u32[]{:S(2)}, u32[]{:S(2)}) collective-permute-start(bf16[1,64,4,2,128]{4,1,3,2,0:T(8,128)(2,1)S(1)} %bitcast.472), channel_id=1, source_target_pairs={{0,4},{4,8},{8,12},{1,5},{5,9},{9,13},{2,6},{6,10},{10,14},{3,7},{... | collective-permute-start | bytes 393224 | tf_op jit(solution)/shard_map/ppermute | solution.py:111
  235.6 8.6 %collective-permute-start.31 = (bf16[1,64,4,2,128]{4,1,3,2,0:T(8,128)(2,1)S(1)}, bf16[1,64,4,2,128]{4,1,3,2,0:T(8,128)(2,1)S(1)}, u32[]{:S(2)}, u32[]{:S(2)}) collective-permute-start(bf16[1,64,4,2,128]{4,1,3,2,0:T(8,128)(2,1)S(1)} %bitcast.474), channel_id=1, source_target_pairs={{0,4},{4,8},{8,12},{1,5},{5,9},{9,13},{2,6},{6,10},{10,14},{3,7},{... | collective-permute-start | bytes 393224 | tf_op jit(solution)/shard_map/ppermute | solution.py:111
  262.4 8.6 %collective-permute-start.35 = (bf16[1,64,4,2,128]{4,1,3,2,0:T(8,128)(2,1)S(1)}, bf16[1,64,4,2,128]{4,1,3,2,0:T(8,128)(2,1)S(1)}, u32[]{:S(2)}, u32[]{:S(2)}) collective-permute-start(bf16[1,64,4,2,128]{4,1,3,2,0:T(8,128)(2,1)S(1)} %bitcast.475), channel_id=1, source_target_pairs={{0,4},{4,8},{8,12},{1,5},{5,9},{9,13},{2,6},{6,10},{10,14},{3,7},{... | collective-permute-start | bytes 393224 | tf_op jit(solution)/shard_map/ppermute | solution.py:111
  288.9 8.6 %collective-permute-start.39 = (bf16[1,64,4,2,128]{4,1,3,2,0:T(8,128)(2,1)S(1)}, bf16[1,64,4,2,128]{4,1,3,2,0:T(8,128)(2,1)S(1)}, u32[]{:S(2)}, u32[]{:S(2)}) collective-permute-start(bf16[1,64,4,2,128]{4,1,3,2,0:T(8,128)(2,1)S(1)} %bitcast.476), channel_id=1, source_target_pairs={{0,4},{4,8},{8,12},{1,5},{5,9},{9,13},{2,6},{6,10},{10,14},{3,7},{... | collective-permute-start | bytes 393224 | tf_op jit(solution)/shard_map/ppermute | solution.py:111
  321.4 51.8 %reduce-scatter.14.cloned.1.call-start = ((), (), s32[]{:S(2)}) async-start(), calls=%async_computation.12 | async-start | bytes 655360 | tf_op jit(solution)/shard_map/reduce_scatter | solution.py:132
  355.9 48.2 %reduce-scatter.16.cloned.1.call-start = ((), (), s32[]{:S(2)}) async-start(), calls=%async_computation.13 | async-start | bytes 655360 | tf_op jit(solution)/shard_map/reduce_scatter | solution.py:132
  386.8 48.1 %reduce-scatter.18.cloned.1.call-start = ((), (), s32[]{:S(2)}) async-start(), calls=%async_computation.14 | async-start | bytes 655360 | tf_op jit(solution)/shard_map/reduce_scatter | solution.py:132
  417.6 47.6 %reduce-scatter.20.cloned.1.call-start = ((), (), s32[]{:S(2)}) async-start(), calls=%async_computation.15 | async-start | bytes 655360 | tf_op jit(solution)/shard_map/reduce_scatter | solution.py:132
  448.0 77.4 %reduce-scatter.22.cloned.1.call-start = ((), (), s32[]{:S(2)}) async-start(), calls=%async_computation.16 | async-start | bytes 655360 | tf_op jit(solution)/shard_map/reduce_scatter | solution.py:132
  465.1 36.9 %collective-permute-start.47 = (bf16[1,64,4,2,128]{4,1,3,2,0:T(8,128)(2,1)}, bf16[1,64,4,2,128]{4,1,3,2,0:T(8,128)(2,1)}, u32[]{:S(2)}, u32[]{:S(2)}) collective-permute-start(bf16[1,64,4,2,128]{4,1,3,2,0:T(8,128)(2,1)} %bitcast.485), channel_id=1, source_target_pairs={{4,0},{8,4},{12,8},{5,1},{9,5},{13,9},{6,2},{10,6},{14,10},{7,3},{... | collective-permute-start | bytes 393224 | tf_op jit(solution)/shard_map/ppermute | solution.py:136
  506.8 61.7 %reduce-scatter.24.cloned.1.call-start = ((), (), s32[]{:S(2)}) async-start(), calls=%async_computation.17 | async-start | bytes 655360 | tf_op jit(solution)/shard_map/reduce_scatter | solution.py:132
  525.5 20.6 %collective-permute-start.48 = (bf16[1,64,4,2,128]{4,1,3,2,0:T(8,128)(2,1)}, bf16[1,64,4,2,128]{4,1,3,2,0:T(8,128)(2,1)S(1)}, u32[]{:S(2)}, u32[]{:S(2)}) collective-permute-start(bf16[1,64,4,2,128]{4,1,3,2,0:T(8,128)(2,1)} %bitcast.487), channel_id=1, source_target_pairs={{4,0},{8,4},{12,8},{5,1},{9,5},{13,9},{6,2},{10,6},{14,10},{7,3},{... | collective-permute-start | bytes 393224 | tf_op jit(solution)/shard_map/ppermute | solution.py:136
  549.9 62.0 %reduce-scatter.26.cloned.1.call-start = ((), (), s32[]{:S(2)}) async-start(), calls=%async_computation.18 | async-start | bytes 655360 | tf_op jit(solution)/shard_map/reduce_scatter | solution.py:132
  568.6 20.9 %collective-permute-start.49 = (bf16[1,64,4,2,128]{4,1,3,2,0:T(8,128)(2,1)}, bf16[1,64,4,2,128]{4,1,3,2,0:T(8,128)(2,1)S(1)}, u32[]{:S(2)}, u32[]{:S(2)}) collective-permute-start(bf16[1,64,4,2,128]{4,1,3,2,0:T(8,128)(2,1)} %bitcast.489), channel_id=1, source_target_pairs={{4,0},{8,4},{12,8},{5,1},{9,5},{13,9},{6,2},{10,6},{14,10},{7,3},{... | collective-permute-start | bytes 393224 | tf_op jit(solution)/shard_map/ppermute | solution.py:136
  593.3 62.3 %reduce-scatter.28.cloned.1.call-start = ((), (), s32[]{:S(2)}) async-start(), calls=%async_computation.19 | async-start | bytes 655360 | tf_op jit(solution)/shard_map/reduce_scatter | solution.py:132
  611.9 21.4 %collective-permute-start.50 = (bf16[1,64,4,2,128]{4,1,3,2,0:T(8,128)(2,1)}, bf16[1,64,4,2,128]{4,1,3,2,0:T(8,128)(2,1)S(1)}, u32[]{:S(2)}, u32[]{:S(2)}) collective-permute-start(bf16[1,64,4,2,128]{4,1,3,2,0:T(8,128)(2,1)} %bitcast.491), channel_id=1, source_target_pairs={{4,0},{8,4},{12,8},{5,1},{9,5},{13,9},{6,2},{10,6},{14,10},{7,3},{... | collective-permute-start | bytes 393224 | tf_op jit(solution)/shard_map/ppermute | solution.py:136
  637.2 62.3 %reduce-scatter.30.cloned.1.call-start = ((), (), s32[]{:S(2)}) async-start(), calls=%async_computation.20 | async-start | bytes 655360 | tf_op jit(solution)/shard_map/reduce_scatter | solution.py:132
  655.7 21.7 %collective-permute-start.51 = (bf16[1,64,4,2,128]{4,1,3,2,0:T(8,128)(2,1)}, bf16[1,64,4,2,128]{4,1,3,2,0:T(8,128)(2,1)S(1)}, u32[]{:S(2)}, u32[]{:S(2)}) collective-permute-start(bf16[1,64,4,2,128]{4,1,3,2,0:T(8,128)(2,1)} %bitcast.493), channel_id=1, source_target_pairs={{4,0},{8,4},{12,8},{5,1},{9,5},{13,9},{6,2},{10,6},{14,10},{7,3},{... | collective-permute-start | bytes 393224 | tf_op jit(solution)/shard_map/ppermute | solution.py:136
  681.2 68.3 %reduce-scatter.32.cloned.1.call-start = ((), (), s32[]{:S(2)}) async-start(), calls=%async_computation.21 | async-start | bytes 655360 | tf_op jit(solution)/shard_map/reduce_scatter | solution.py:132
  699.6 20.7 %collective-permute-start.52 = (bf16[1,64,4,2,128]{4,1,3,2,0:T(8,128)(2,1)}, bf16[1,64,4,2,128]{4,1,3,2,0:T(8,128)(2,1)S(1)}, u32[]{:S(2)}, u32[]{:S(2)}) collective-permute-start(bf16[1,64,4,2,128]{4,1,3,2,0:T(8,128)(2,1)} %bitcast.495), channel_id=1, source_target_pairs={{4,0},{8,4},{12,8},{5,1},{9,5},{13,9},{6,2},{10,6},{14,10},{7,3},{... | collective-permute-start | bytes 393224 | tf_op jit(solution)/shard_map/ppermute | solution.py:136
  (98 other events, 893.3 us)
Sparse Core Ops, SparseCore 0:
  321.5 20.8 reduce-scatter.11
  356.0 17.1 reduce-scatter.13
  386.9 17.0 reduce-scatter.15
  417.7 17.1 reduce-scatter.17
  448.1 16.9 reduce-scatter.19
  506.9 17.7 reduce-scatter.21
  550.0 17.8 reduce-scatter.23
  593.4 17.8 reduce-scatter.25
  637.3 17.9 reduce-scatter.27
  681.3 18.0 reduce-scatter.29
  724.6 17.9 reduce-scatter.31
